TPU v7x, 1024 devices: a whole 4x4x32 slice. The times are simulated.
1024 devices in a mesh: seq: 64 (over z, x_hi), fsdp: 16 (over x_lo, y, core).
Axes of the slice: x: 4 (x_hi: 2, x_lo: 2; x = x_hi * 2 + x_lo), y: 4, z: 32, core: 2. Of those that a mesh axis runs over, the one named last changes fastest.
Arguments:
- projected: bfloat16 [3, 8192, 32768], P(None, 'fsdp', 'seq'), may hold values from -6 to 6
- short_weight: float32 [3, 8192, 3], P(None, 'fsdp'), may hold values from -3.5 to 3.5
- skip_weight: float32 [8192], P('fsdp'), may hold values from -4 to 4
- decay_rates: float32 [8192, 16], P('fsdp'), may hold values from 1.5258789e-05 to 0.05
- residues: float32 [8192, 16], P('fsdp'), may hold values from -1.5 to 1.5
Outputs:
- output: bfloat16 [8192, 32768], P('fsdp', 'seq')
All inputs are finite; a program needn't handle non-finite values.
Results may differ from a plain program's by a relative error of at most 0.0058.
Values may be sent and summed in bfloat16 or wider, within the bound.
No kernel may reach another device: no remote copies, remote signals or barrier semaphores. Data moves between devices by JAX's collectives and lax.ppermute only.
A program may use at most 64 MiB of HBM per device.

v0:
```python
import math

import jax
import jax.numpy as jnp
from jax import lax
from jax.sharding import PartitionSpec as P


def from_behind(value, axis, steps):
    count = lax.axis_size(axis)
    leading, last = (max(0, -steps), min(count, count - steps))
    return lax.ppermute(value, axis, [(source, source + steps) for source in range(leading, last)])


def combine(earlier, later):
    return (earlier[0] * later[0], later[0] * earlier[1] + later[1])


def modal_block(signal, weight, decay_rate, initial):
    channels, length = signal.shape
    block_len = min(128, length)
    block_count = length // block_len
    offsets = jnp.arange(block_len, dtype=jnp.float32)
    falloff = jnp.exp(-decay_rate[:, :, None] * offsets)
    filter_taps = jnp.einsum("gk,gkb->gb", weight, falloff, precision=lax.Precision.HIGHEST)
    positions = jnp.arange(block_len, dtype=jnp.int32)
    lag_index = positions[:, None] - positions[None, :]
    toeplitz = jnp.where(lag_index >= 0, filter_taps[:, jnp.maximum(lag_index, 0)], 0.0)
    sliced = signal.reshape(channels, block_count, block_len)
    inside = jnp.einsum("gij,gnj->gni", toeplitz, sliced, precision=lax.Precision.HIGHEST)
    entering = jnp.exp(-decay_rate[:, :, None] * (block_len - offsets))
    block_ends = jnp.einsum("gkj,gnj->gkn", entering, sliced, precision=lax.Precision.HIGHEST)
    decays = jnp.broadcast_to(jnp.exp(-decay_rate * block_len)[:, :, None], block_ends.shape)
    powers, partial_sums = lax.associative_scan(combine, (decays, block_ends), axis=2)
    states_after = powers * initial[:, :, None] + partial_sums
    states = jnp.concatenate([initial[:, :, None], states_after[:, :, :-1]], axis=2)
    carried = jnp.einsum(
        "gkb,gkn->gnb", weight[:, :, None] * falloff, states, precision=lax.Precision.HIGHEST
    )
    return ((inside + carried).reshape(channels, length), states_after[:, :, -1])


def grouped(signal, weight, decay_rate, initial):
    channels, length = signal.shape
    group = math.gcd(channels, 64)
    count = channels // group
    pieces = (
        signal.reshape(count, group, length),
        weight.reshape(count, group, -1),
        decay_rate.reshape(count, group, -1),
        initial.reshape(count, group, -1),
    )

    def apply_one(item):
        return modal_block(item[0], item[1], item[2], item[3])

    results, finals = lax.map(apply_one, pieces)
    return (results.reshape(channels, length), finals.reshape(channels, -1))


def shards(projected, short_weight, skip_weight, decay_rates, residues):
    taps_count = short_weight.shape[2]
    channels = projected.shape[1]
    length = projected.shape[2]
    tail = jnp.swapaxes(projected[:, :, length - (taps_count - 1) :], 1, 2)
    before = from_behind(tail, "seq", 1)
    padded = jnp.concatenate([jnp.swapaxes(before, 1, 2), projected], axis=2).astype(jnp.float32)
    feats = jnp.zeros((3, channels, length), jnp.float32)
    for lag in range(taps_count):
        begin = taps_count - 1 - lag
        feats = feats + short_weight[:, :, lag][:, :, None] * padded[:, :, begin : begin + length]
    mixed = (feats[1] * feats[2]).astype(jnp.bfloat16)
    mixed = lax.optimization_barrier(mixed)
    owned = channels // lax.axis_size("seq")
    first = lax.axis_index("seq") * owned
    decay_rate = lax.dynamic_slice_in_dim(decay_rates, first, owned, 0)
    residue = lax.dynamic_slice_in_dim(residues, first, owned, 0)
    weight = residue * jnp.sqrt(2.0 * decay_rate)
    gains = lax.dynamic_slice_in_dim(skip_weight, first, owned, 0)
    regrouped = lax.all_to_all(mixed, "seq", split_axis=0, concat_axis=1, tiled=True)
    signal = regrouped.astype(jnp.float32)
    zeros_state = jnp.zeros(decay_rate.shape, jnp.float32)
    convolved, unused = grouped(signal, weight, decay_rate, zeros_state)
    summed = (convolved + gains[:, None] * signal).astype(jnp.bfloat16)
    summed = lax.all_to_all(summed, "seq", split_axis=1, concat_axis=0, tiled=True)
    return (feats[0] * summed.astype(jnp.float32)).astype(jnp.bfloat16)


def solution(mesh):
    return jax.shard_map(
        shards,
        mesh=mesh,
        in_specs=(
            P(None, "fsdp", "seq"),
            P(None, "fsdp", None),
            P("fsdp"),
            P("fsdp", None),
            P("fsdp", None),
        ),
        out_specs=P("fsdp", "seq"),
        check_vma=False,
    )
```

profile of v0, /device:TPU:14, one launch (start us, length us, event | category | flops | bytes accessed | tf_op | source)
XLA Modules:
  0.0 398.8 jit_solution(4456673670391103096)
XLA Ops:
  1.2 4.7 %collective-permute-start = (bf16[3,2,512]{1,2,0:T(8,128)(2,1)S(1)}, bf16[3,2,512]{1,2,0:T(8,128)(2,1)S(1)}, u32[]{:S(2)}, u32[]{:S(2)}) collective-permute-start(bf16[3,2,512]{1,2,0:T(8,128)(2,1)S(1)} %slice_bitcast_fusion.1), channel_id=1, source_target_pairs={{0,16},{16,32},{32,48},{48,64},{64,80},{80,96},{96,112},{112,128},... | collective-permute-start | bytes 18440 | tf_op jit(solution)/shard_map/ppermute | solution.py:12
  6.7 8.7 %collective-permute-done = bf16[3,2,512]{1,2,0:T(8,128)(2,1)S(1)} collective-permute-done((bf16[3,2,512]{1,2,0:T(8,128)(2,1)S(1)}, bf16[3,2,512]{1,2,0:T(8,128)(2,1)S(1)}, u32[]{:S(2)}, u32[]{:S(2)}) %collective-permute-start) | collective-permute-done | bytes 6176 | tf_op jit(solution)/shard_map/ppermute | solution.py:12
  15.4 2.2 maximum_convert_fusion
  17.7 2.8 fusion
  21.4 32.6 %all-to-all-start = ((bf16[64,8,512]{2,1,0:T(8,128)(2,1)}), bf16[64,8,512]{2,1,0:T(8,128)(2,1)}, u32[]{:S(2)}, u32[]{:S(2)}) async-start(bf16[64,8,512]{2,1,0:T(8,128)(2,1)} %bitcast.63), calls=%async_computation | async-start | bytes 1048576 | tf_op jit(solution)/shard_map/all_to_all | solution.py:80
  56.0 54.8 %gather_fusion = f32[16384,8]{1,0:T(8,128)} fusion(f32[8,128]{0,1:T(8,128)S(1)} %bitcast.61, s32[16384]{0:T(1024)S(1)} %bitcast_clamp_fusion), kind=kCustom, calls=%fused_computation | custom fusion | bytes 1114112 | tf_op jit(solution)/shard_map/while/body/eval_jaxpr/gather | solution.py:28
  110.8 5.9 %copy.68 = f32[128,128,8]{1,0,2:T(8,128)} copy(f32[128,128,8]{2,1,0:T(8,128)} %bitcast.62) | data formatting | bytes 1048576 | tf_op jit(solution)/shard_map/while/body/eval_jaxpr/gather | solution.py:28
  123.5 3.4 pad.135
  126.9 2.0 copy.65
  128.9 2.2 reshape.80
  131.1 1.6 fusion.20
  132.7 2.2 slice.356
  134.9 2.2 slice.355
  149.9 1.7 add_multiply_fusion.13
  152.3 1.6 fusion.38
  156.8 1.7 slice.394
  158.5 3.9 slice.396
  162.5 1.6 pad_maximum_fusion
  164.1 3.1 pad.134
  167.8 1.5 add.221
  169.3 3.2 pad.137
  172.5 4.9 %pad.151 = f32[8,16,4]{2,1,0:T(8,128)} pad(f32[8,16,2]{2,1,0:T(8,128)} %pad_add_fusion, f32[]{:T(128)} %constant.37.clone.1), padding=0_0_0x0_0_0x1_0_1 | pad | bytes 3076 | tf_op jit(solution)/shard_map/while/body/eval_jaxpr/pad | solution.py:34
  177.4 1.6 pad_maximum_fusion.7
  179.0 4.9 %pad.150 = f32[8,16,4]{2,1,0:T(8,128)} pad(f32[8,16,2]{2,1,0:T(8,128)} %pad_maximum_fusion.7, f32[]{:T(128)} %constant.37.clone.1), padding=0_0_0x0_0_0x0_1_1 | pad | bytes 3076 | tf_op jit(solution)/shard_map/while/body/eval_jaxpr/pad | solution.py:34
  183.8 1.5 add.238
  185.4 1.7 add_multiply_fusion.12
  187.0 1.5 pad_maximum_fusion.1
  188.6 4.9 %pad.136 = f32[8,16,8]{2,1,0:T(8,128)} pad(f32[8,16,4]{2,1,0:T(8,128)} %pad_maximum_fusion.1, f32[]{:T(128)} %constant.37.clone.1), padding=0_0_0x0_0_0x0_1_1 | pad | bytes 6148 | tf_op jit(solution)/shard_map/while/body/eval_jaxpr/pad | solution.py:34
  193.5 4.9 %pad.153 = f32[8,16,8]{2,1,0:T(8,128)} pad(f32[8,16,4]{2,1,0:T(8,128)} %add.238, f32[]{:T(128)} %constant.37.clone.1), padding=0_0_0x0_0_0x1_0_1 | pad | bytes 6148 | tf_op jit(solution)/shard_map/while/body/eval_jaxpr/pad | solution.py:34
  198.4 1.5 pad_maximum_fusion.8
  199.9 3.2 pad.152
  206.0 1.6 add_multiply_fusion.11
  209.3 3.2 pad.139
  213.8 3.3 pad.141
  217.1 5.0 %pad.155 = f32[8,16,16]{2,1,0:T(8,128)} pad(f32[8,16,8]{2,1,0:T(8,128)} %add.240, f32[]{:T(128)} %constant.37.clone.1), padding=0_0_0x0_0_0x1_0_1 | pad | bytes 12292 | tf_op jit(solution)/shard_map/while/body/eval_jaxpr/pad | solution.py:34
  222.0 1.5 pad_maximum_fusion.9
  223.6 3.2 pad.154
  228.2 1.6 add_multiply_fusion.10
  229.9 1.5 pad_maximum_fusion.3
  231.4 3.3 pad.140
  234.7 5.0 %pad.157 = f32[8,16,32]{2,1,0:T(8,128)} pad(f32[8,16,16]{2,1,0:T(8,128)} %add.242, f32[]{:T(128)} %constant.37.clone.1), padding=0_0_0x0_0_0x1_0_1 | pad | bytes 24580 | tf_op jit(solution)/shard_map/while/body/eval_jaxpr/pad | solution.py:34
  239.8 1.5 pad_maximum_fusion.10
  241.3 3.3 pad.156
  245.2 1.5 add.244
  246.7 1.6 add_multiply_fusion.9
  250.3 3.5 pad.143
  254.4 3.8 pad.145
  258.2 5.1 %pad.159 = f32[8,16,64]{2,1,0:T(8,128)} pad(f32[8,16,32]{2,1,0:T(8,128)} %add.244, f32[]{:T(128)} %constant.37.clone.1), padding=0_0_0x0_0_0x1_0_1 | pad | bytes 49156 | tf_op jit(solution)/shard_map/while/body/eval_jaxpr/pad | solution.py:34
  263.3 1.6 pad_maximum_fusion.11
  264.9 3.4 pad.158
  268.3 1.5 add.246
  269.8 1.6 add_multiply_fusion.8
  272.3 1.6 pad.144
  273.9 3.8 pad.161
  278.6 1.6 pad.160
  282.6 2.7 pad.198
  286.2 2.7 pad.196
  288.9 4.5 %pad.239 = f32[8,16,256]{2,1,0:T(8,128)S(1)} pad(f32[8,16,128]{2,1,0:T(8,128)} %add.226, f32[]{:T(128)} %constant.37.clone.1), padding=0_0_0x0_0_0x1_0_1 | pad | bytes 196612
  293.3 6.0 %pad.238 = f32[8,16,256]{2,1,0:T(8,128)} pad(f32[8,16,128]{2,1,0:T(8,128)} %add.248, f32[]{:T(128)} %constant.37.clone.1), padding=0_0_0x0_0_0x1_0_1 | pad | bytes 196612
  299.4 1.8 fusion.7
  302.1 3.6 convolution_add_fusion
  305.7 2.3 reshape.81
  308.1 2.0 fusion.5
  310.0 87.9 %all_to_all.26 = bf16[8,64,512]{2,0,1:T(8,128)(2,1)S(1)} all-to-all(bf16[8,64,512]{2,0,1:T(8,128)(2,1)S(1)} %fusion.5), channel_id=1, replica_groups=mesh['seq'=64,'fsdp'=16] {'seq'}, dimensions={1} | all-to-all | bytes 1048576 | tf_op jit(solution)/shard_map/all_to_all | solution.py:85
  (95 shorter events, 46.2 us)
Async XLA Ops:
  1.2 14.3 %collective-permute-start = (bf16[3,2,512]{1,2,0:T(8,128)(2,1)S(1)}, bf16[3,2,512]{1,2,0:T(8,128)(2,1)S(1)}, u32[]{:S(2)}, u32[]{:S(2)}) collective-permute-start(bf16[3,2,512]{1,2,0:T(8,128)(2,1)S(1)} %slice_bitcast_fusion.1), channel_id=1, source_target_pairs={{0,16},{16,32},{32,48},{48,64},{64,80},{80,96},{96,112},{112,128},... | collective-permute-start | bytes 18440 | tf_op jit(solution)/shard_map/ppermute | solution.py:12
  21.4 105.5 %all-to-all-start = ((bf16[64,8,512]{2,1,0:T(8,128)(2,1)}), bf16[64,8,512]{2,1,0:T(8,128)(2,1)}, u32[]{:S(2)}, u32[]{:S(2)}) async-start(bf16[64,8,512]{2,1,0:T(8,128)(2,1)} %bitcast.63), calls=%async_computation | async-start | bytes 1048576 | tf_op jit(solution)/shard_map/all_to_all | solution.py:80
  55.6 61.1 %copy-start.10 = (f32[8,16]{1,0:T(8,128)}, f32[8,16]{1,0:T(8,128)S(1)}, u32[]{:S(2)}) copy-start(f32[8,16]{1,0:T(8,128)S(1)} %get-tuple-element.45) | copy-start | bytes 1540
  55.6 75.5 %copy-start.6 = (f32[8,16]{1,0:T(8,128)}, f32[8,16]{1,0:T(8,128)S(1)}, u32[]{:S(2)}) copy-start(f32[8,16]{1,0:T(8,128)S(1)} %get-tuple-element.44) | copy-start | bytes 1540
  55.6 81.5 %copy-start.7 = (f32[8,16]{1,0:T(8,128)}, f32[8,16]{1,0:T(8,128)S(1)}, u32[]{:S(2)}) copy-start(f32[8,16]{1,0:T(8,128)S(1)} %get-tuple-element.43) | copy-start | bytes 1540
  55.6 83.9 %copy-start.8 = (f32[8,16]{1,0:T(8,128)}, f32[8,16]{1,0:T(8,128)S(1)}, u32[]{:S(2)}) copy-start(f32[8,16]{1,0:T(8,128)S(1)} %get-tuple-element.36) | copy-start | bytes 1540
  55.6 85.2 %copy-start.9 = (f32[8,16]{1,0:T(8,128)}, f32[8,16]{1,0:T(8,128)S(1)}, u32[]{:S(2)}) copy-start(f32[8,16]{1,0:T(8,128)S(1)} %get-tuple-element.37) | copy-start | bytes 1540
  117.5 11.4 %copy-start.4 = (f32[8,16,1]{2,1,0:T(8,128)}, f32[8,16,1]{2,1,0:T(8,128)S(1)}, u32[]{:S(2)}) copy-start(f32[8,16,1]{2,1,0:T(8,128)S(1)} %copy.70) | copy-start | bytes 1540
  117.6 11.3 %copy-start.5 = (f32[8,16,1]{2,1,0:T(8,128)}, f32[8,16,1]{2,1,0:T(8,128)S(1)}, u32[]{:S(2)}) copy-start(f32[8,16,1]{2,1,0:T(8,128)S(1)} %copy.69) | copy-start | bytes 1540
  132.7 4.5 %copy-start = (f32[8,16,256]{2,1,0:T(8,128)}, f32[8,16,256]{2,1,0:T(8,128)S(1)}, u32[]{:S(2)}) copy-start(f32[8,16,256]{2,1,0:T(8,128)S(1)} %fusion.20) | copy-start | bytes 393220
  167.2 0.6 copy-start.2
  209.2 4.5 %copy-start.1 = (f32[8,16,16]{2,1,0:T(8,128)}, f32[8,16,16]{2,1,0:T(8,128)S(1)}, u32[]{:S(2)}) copy-start(f32[8,16,16]{2,1,0:T(8,128)S(1)} %pad.138) | copy-start | bytes 24580
  212.5 0.6 copy-start.3
  217.1 65.4 %slice-start = ((f32[8,16,256]{2,1,0:T(8,128)}), f32[8,16,1]{2,1,0:T(8,128)S(1)}, s32[]{:S(2)}) async-start(f32[8,16,256]{2,1,0:T(8,128)} %copy-done), calls=%async_computation.2 | async-start | bytes 131072 | tf_op jit(solution)/shard_map/while/body/eval_jaxpr/slice | solution.py:34
  301.2 6.9 %copy-start.11 = (f32[8]{0:T(128)S(1)}, f32[8]{0:T(128)}, u32[]{:S(2)}) copy-start(f32[8]{0:T(128)} %dynamic_slice.21) | copy-start | bytes 100
where the time goes:
time: 406 us; the launch traced here: 399 us
  local copies, waits for them, and re-layouts  199 us (49%)
  blocking collectives  87.9 us (22%)
  other arithmetic  58 us (14%)
  starting transfers between devices  37.3 us (9%)
  waiting for transfers between devices  8.68 us (2%)
  matrix products  7.27 us (2%)
    all_to_all x1, blocking collectives, shards(): lax.all_to_all(summed, 'seq', split_axis=1, concat_axis=0, tiled=True)  87.9 us
    pad x24, local copies, waits for them, and re-layouts, modal_block(): lax.associative_scan(combine, (decays, block_ends), axis=2)  83.2 us
    gather x2, local copies, waits for them, and re-layouts, modal_block(): filter_taps[:, jnp.maximum(lag_index, 0)]  60.6 us
    all_to_all x1, starting transfers between devices, shards(): lax.all_to_all(mixed, 'seq', split_axis=0, concat_axis=1, tiled=True)  32.6 us
    slice x30, local copies, waits for them, and re-layouts, modal_block(): lax.associative_scan(combine, (decays, block_ends), axis=2)  27.3 us
    concatenate x14, other arithmetic, modal_block(): lax.associative_scan(combine, (decays, block_ends), axis=2)  17.1 us
    add x14, other arithmetic, modal_block(): lax.associative_scan(combine, (decays, block_ends), axis=2)  14.3 us
    unnamed x30, local copies, waits for them, and re-layouts  11.9 us
  transfers between devices with their start and end apart: 2, of which 1 were waited for; matrix products, arithmetic and copies ran while one was open for 18% of the time, Pallas kernels for 0%

commit v1 on v0

v1 whole, which is shorter than its diff:
```python
import jax
import jax.numpy as jnp
from jax import lax
from jax.sharding import PartitionSpec as P


def from_behind(value, axis, steps):
    count = lax.axis_size(axis)
    leading, last = (max(0, -steps), min(count, count - steps))
    return lax.ppermute(value, axis, [(source, source + steps) for source in range(leading, last)])


def short_conv(projected, short_weight):
    taps_count = short_weight.shape[2]
    length = projected.shape[2]
    tail = jnp.swapaxes(projected[:, :, length - (taps_count - 1) :], 1, 2)
    before = from_behind(tail, "seq", 1)
    padded = jnp.concatenate([jnp.swapaxes(before, 1, 2), projected], axis=2).astype(jnp.float32)
    feats = jnp.zeros(projected.shape, jnp.float32)
    for lag in range(taps_count):
        begin = taps_count - 1 - lag
        feats = feats + short_weight[:, :, lag][:, :, None] * padded[:, :, begin : begin + length]
    return feats


def shards(projected, short_weight, skip_weight, decay_rates, residues):
    channels = projected.shape[1]
    length = projected.shape[2]
    modes = decay_rates.shape[1]
    feats = short_conv(projected, short_weight)
    mixed = (feats[1] * feats[2]).astype(jnp.bfloat16)
    signal = mixed.astype(jnp.float32)

    block = min(128, length)
    count = length // block
    rate = decay_rates
    weight = residues * jnp.sqrt(2.0 * rate)
    offsets = jnp.arange(block, dtype=jnp.float32)
    rising = jnp.exp(rate[:, :, None] * offsets)
    falling = weight[:, :, None] * jnp.exp(-rate[:, :, None] * offsets)

    blocks = signal.reshape(channels, 1, count, block)
    scaled = blocks * rising[:, :, None, :]
    high = scaled.astype(jnp.bfloat16)
    low = (scaled - high.astype(jnp.float32)).astype(jnp.bfloat16)
    rows = jnp.arange(block)
    ones = (rows[:, None] <= rows[None, :]).astype(jnp.bfloat16)
    pair = jnp.concatenate([high, low], axis=3)
    stacked = jnp.concatenate([ones, ones], axis=0)
    running = jnp.einsum("ckni,ij->cknj", pair, stacked, preferred_element_type=jnp.float32)

    block_sums = jnp.sum(scaled, axis=3) * jnp.exp(-rate * (block - 1))[:, :, None]
    step = jnp.exp(-rate * block)
    carried = [jnp.zeros_like(rate)]
    for n in range(count):
        carried.append(step * carried[-1] + block_sums[:, :, n])
    local_final = carried[-1]
    local_states = jnp.stack(carried[:count], axis=2)

    gathered = lax.all_gather(local_final, "seq")
    devices = gathered.shape[0]
    here = lax.axis_index("seq")
    others = jnp.arange(devices)
    distance = here - 1 - others
    decay_between = jnp.exp(
        -rate[None, :, :] * (length * jnp.maximum(distance, 0)).astype(jnp.float32)[:, None, None]
    )
    decay_between = jnp.where((others < here)[:, None, None], decay_between, 0.0)
    incoming = jnp.sum(decay_between * gathered, axis=0)

    starts = (jnp.arange(count) * block + 1).astype(jnp.float32)
    entering = jnp.exp(-rate)[:, :, None] * local_states + jnp.exp(-rate[:, :, None] * starts) * incoming[:, :, None]
    convolved = jnp.sum(falling[:, :, None, :] * (running + entering[:, :, :, None]), axis=1)
    convolved = convolved.reshape(channels, length)
    summed = (convolved + skip_weight[:, None] * signal).astype(jnp.bfloat16)
    return (feats[0] * summed.astype(jnp.float32)).astype(jnp.bfloat16)


def solution(mesh):
    return jax.shard_map(
        shards,
        mesh=mesh,
        in_specs=(
            P(None, "fsdp", "seq"),
            P(None, "fsdp", None),
            P("fsdp"),
            P("fsdp", None),
            P("fsdp", None),
        ),
        out_specs=P("fsdp", "seq"),
        check_vma=False,
    )
```

time: 406 us -> 346 us (0.85)
  the two profiles are of different devices: /device:TPU:14 before, /device:TPU:8 now
where the time goes in v1:
time: 346 us; the launch traced here: 345 us
  waiting for transfers between devices  280 us (81%)
  other arithmetic  24.2 us (7%)
  between operations  13.5 us (4%)
  local copies, waits for them, and re-layouts  12.8 us (4%)
  matrix products  10.1 us (3%)
  starting transfers between devices  4.93 us (1%)
    all_gather x1, waiting for transfers between devices, shards(): gathered = lax.all_gather(local_final, 'seq')  280 us
    dot_general x1, matrix products, shards(): jnp.einsum('ckni,ij->cknj', pair, stacked, preferred_element_type=jnp.flo...  10.1 us
    reduce_sum x1, other arithmetic, shards(): jnp.sum(scaled, axis=3) * jnp.exp(-rate * (block - 1))[:, :, None]  10 us
  transfers between devices with their start and end apart: 2, of which 1 were waited for; matrix products, arithmetic and copies ran while one was open for 3% of the time, Pallas kernels for 0%

profile of v1, /device:TPU:8, one launch (start us, length us, event | category | flops | bytes accessed | tf_op | source)
XLA Modules:
  0.0 345.5 jit_solution(1104706111522553206)
XLA Ops:
  6.5 0.0 copy-start.1
  6.5 0.0 copy-start.2
  6.5 0.0 all-gather.3.cloned.1.call-start
  6.5 1.7 copy.24
  8.3 4.9 %collective-permute-start = (bf16[3,2,512]{2,1,0:T(2,128)(2,1)S(1)}, bf16[3,2,512]{2,1,0:T(2,128)(2,1)S(1)}, u32[]{:S(2)}, u32[]{:S(2)}) collective-permute-start(bf16[3,2,512]{2,1,0:T(2,128)(2,1)S(1)} %slice_bitcast_fusion.5), channel_id=1, source_target_pairs={{0,16},{16,32},{32,48},{48,64},{64,80},{80,96},{96,112},{112,128},... | collective-permute-start | bytes 18440 | tf_op jit(solution)/shard_map/ppermute | solution.py:10
  13.2 0.9 fusion.28
  14.1 3.9 %multiply_exponential_fusion = f32[512,16,128]{2,0,1:T(8,128)} fusion(f32[512,16]{0,1:T(8,128)} %param.8), kind=kLoop, calls=%fused_computation.9 | loop fusion | flops 1048576 | bytes 4227072 | tf_op jit(solution)/shard_map/exp | solution.py:39
  18.0 0.0 copy-done.1
  18.0 0.0 copy-done.2
  18.0 0.0 collective-permute-done
  18.0 0.5 maximum_convert_fusion
  18.5 0.9 fusion.7
  19.4 1.2 fusion.15
  20.6 2.5 copy.26
  23.2 10.0 %multiply_reduce_fusion = (f32[512,16,4]{0,2,1:T(4,128)S(1)}, bf16[512,16,4,128]{3,0,2,1:T(8,128)(2,1)}, bf16[512,16,4,128]{3,0,2,1:T(8,128)(2,1)}) fusion(f32[512,16,128]{2,0,1:T(8,128)} %multiply_exponential_fusion, f32[512,4,128]{2,0,1:T(8,128)} %copy.26), kind=kLoop, calls=%fused_computation | loop fusion | flops 25133056 | bytes 22151168 | tf_op jit(solution)/shard_map/reduce_sum | solution.py:52
  33.2 0.6 fusion.19
  33.9 0.0 all-gather.3.cloned.1.call-update
  34.0 3.8 %exponential_multiply_fusion = f32[512,16,128]{2,0,1:T(8,128)} fusion(f32[512,16]{0,1:T(8,128)S(1)} %get-tuple-element.15, f32[512,16]{0,1:T(8,128)S(1)} %get-tuple-element.12), kind=kLoop, calls=%fused_computation.10 | loop fusion | flops 2097152 | bytes 4259840 | tf_op jit(solution)/shard_map/mul | solution.py:40
  37.8 279.9 %all-gather.3.cloned.1.call-done = f32[32768,16]{0,1:T(8,128)} async-done(((f32[512,16]{0,1:T(8,128)}), f32[32768,16]{0,1:T(8,128)}) %all-gather.3.cloned.1.call-update) | async-done | bytes 2097168 | tf_op jit(solution)/shard_map/all_gather | solution.py:60
  317.7 0.0 copy-start
  317.7 3.0 copy.35
  320.7 0.5 fusion.9
  321.2 0.1 fusion.16
  321.3 0.1 copy.28
  321.4 0.0 copy-done
  321.4 0.0 copy-start.3
  321.4 10.1 %multiply_reduce_fusion.1 = f32[512,4,128]{2,0,1:T(8,128)} fusion(bf16[512,16,4,128]{3,0,2,1:T(8,128)(2,1)} %get-tuple-element.6, bf16[512,16,4,128]{3,0,2,1:T(8,128)(2,1)} %get-tuple-element.7, f32[512,16,4]{0,2,1:T(4,128)S(1)} %copy.28, f32[512,16,128]{2,0,1:T(8,128)S(1)} %copy-done, pred[128,128]{1,0:T(32,128)(4,1)S(1)} %iota_compare_fusion), kind=kOutput, calls=%fused_computation.8 | convolution fusion | flops 2193391616 | bytes 22167552 | tf_op jit(solution)/shard_map/ckni,ij->cknj/dot_general | solution.py:50
  331.5 2.5 copy.29
  334.0 0.0 copy-done.3
  334.0 2.5 fusion.12
  336.6 2.0 copy.30
  (10 shorter events, 0.1 us)
Async XLA Ops:
  6.5 11.4 %copy-start.1 = (f32[512,16]{0,1:T(8,128)S(1)}, f32[512,16]{0,1:T(8,128)}, u32[]{:S(2)}) copy-start(f32[512,16]{0,1:T(8,128)} %param.8) | copy-start | bytes 98308
  6.5 11.4 %copy-start.2 = (f32[512,16]{0,1:T(8,128)S(1)}, f32[512,16]{0,1:T(8,128)}, u32[]{:S(2)}) copy-start(f32[512,16]{0,1:T(8,128)} %param.9) | copy-start | bytes 98308
  6.5 311.2 %all-gather.3.cloned.1.call-start = ((), (), s32[]{:S(2)}) async-start(), calls=%async_computation | async-start | bytes 2129920 | tf_op jit(solution)/shard_map/all_gather | solution.py:60
  8.3 9.7 %collective-permute-start = (bf16[3,2,512]{2,1,0:T(2,128)(2,1)S(1)}, bf16[3,2,512]{2,1,0:T(2,128)(2,1)S(1)}, u32[]{:S(2)}, u32[]{:S(2)}) collective-permute-start(bf16[3,2,512]{2,1,0:T(2,128)(2,1)S(1)} %slice_bitcast_fusion.5), channel_id=1, source_target_pairs={{0,16},{16,32},{32,48},{48,64},{64,80},{80,96},{96,112},{112,128},... | collective-permute-start | bytes 18440 | tf_op jit(solution)/shard_map/ppermute | solution.py:10
  317.7 3.7 %copy-start = (f32[512,16,128]{2,0,1:T(8,128)S(1)}, f32[512,16,128]{2,0,1:T(8,128)}, u32[]{:S(2)}) copy-start(f32[512,16,128]{2,0,1:T(8,128)} %exponential_multiply_fusion) | copy-start | bytes 12582916
  321.4 12.6 %copy-start.3 = (f32[512]{0:T(512)S(1)}, f32[512]{0:T(512)}, u32[]{:S(2)}) copy-start(f32[512]{0:T(512)} %param.7) | copy-start | bytes 6148
Sparse Core Ops, SparseCore 0:
  34.0 283.6 all-gather.2

commit v2 on v1

--- a/solution.py
+++ b/solution.py
@@ -21,6 +21,18 @@
         begin = taps_count - 1 - lag
         feats = feats + short_weight[:, :, lag][:, :, None] * padded[:, :, begin : begin + length]
     return feats
+
+
+def scan_states(final, rate, length):
+    count = lax.axis_size("seq")
+    acc = from_behind(final, "seq", 1)
+    if count > 2:
+        acc = acc + jnp.exp(-rate * length) * from_behind(final, "seq", 2)
+    shift = 2
+    while shift < count:
+        acc = acc + jnp.exp(-rate * float(length * shift)) * from_behind(acc, "seq", shift)
+        shift *= 2
+    return acc
 
 
 def shards(projected, short_weight, skip_weight, decay_rates, residues):
@@ -57,20 +69,13 @@
     local_final = carried[-1]
     local_states = jnp.stack(carried[:count], axis=2)
 
-    gathered = lax.all_gather(local_final, "seq")
-    devices = gathered.shape[0]
-    here = lax.axis_index("seq")
-    others = jnp.arange(devices)
-    distance = here - 1 - others
-    decay_between = jnp.exp(
-        -rate[None, :, :] * (length * jnp.maximum(distance, 0)).astype(jnp.float32)[:, None, None]
-    )
-    decay_between = jnp.where((others < here)[:, None, None], decay_between, 0.0)
-    incoming = jnp.sum(decay_between * gathered, axis=0)
+    incoming = scan_states(local_final, rate, length)
 
+    local_part = jnp.exp(-rate)[:, :, None] * local_states
+    convolved = jnp.sum(falling[:, :, None, :] * (running + local_part[:, :, :, None]), axis=1)
     starts = (jnp.arange(count) * block + 1).astype(jnp.float32)
-    entering = jnp.exp(-rate)[:, :, None] * local_states + jnp.exp(-rate[:, :, None] * starts) * incoming[:, :, None]
-    convolved = jnp.sum(falling[:, :, None, :] * (running + entering[:, :, :, None]), axis=1)
+    entering = jnp.exp(-rate[:, :, None] * starts) * incoming[:, :, None]
+    convolved = convolved + jnp.sum(falling[:, :, None, :] * entering[:, :, :, None], axis=1)
     convolved = convolved.reshape(channels, length)
     summed = (convolved + skip_weight[:, None] * signal).astype(jnp.bfloat16)
     return (feats[0] * summed.astype(jnp.float32)).astype(jnp.bfloat16)

time: 346 us -> 127 us (0.37)
  the two profiles are of different devices: /device:TPU:8 before, /device:TPU:14 now
where the time goes in v2:
time: 127 us
  starting transfers between devices  75.7 us (60%)
  other arithmetic  24.4 us (19%)
  waiting for transfers between devices  9.42 us (7%)
  local copies, waits for them, and re-layouts  8.96 us (7%)
  matrix products  7.9 us (6%)
    ppermute x8, starting transfers between devices, from_behind(): lax.ppermute(value, axis, [(source, source + steps) for source in range(l...  75.7 us
    ppermute x8, waiting for transfers between devices, from_behind(): lax.ppermute(value, axis, [(source, source + steps) for source in range(l...  9.42 us
    dot_general x1, matrix products, shards(): jnp.einsum('ckni,ij->cknj', pair, stacked, preferred_element_type=jnp.flo...  7.9 us
    reduce_sum x1, other arithmetic, shards(): jnp.sum(scaled, axis=3) * jnp.exp(-rate * (block - 1))[:, :, None]  6.41 us
    reduce_sum x1, other arithmetic, shards(): jnp.sum(falling[:, :, None, :] * entering[:, :, :, None], axis=1)  5.08 us
    exp x1, other arithmetic, shards(): rising = jnp.exp(rate[:, :, None] * offsets)  3.87 us
  transfers between devices with their start and end apart: 8, of which 6 were waited for; matrix products, arithmetic and copies ran while one was open for 3% of the time, Pallas kernels for 0%

profile of v2, /device:TPU:14, one launch (start us, length us, event | category | flops | bytes accessed | tf_op | source)
XLA Modules:
  0.0 126.6 jit_solution(12024674729363620269)
XLA Ops:
  0.0 0.0 copy-start
  0.0 0.0 copy-start.2
  0.0 1.7 %copy.24 = bf16[3,512,512]{1,2,0:T(8,128)(2,1)S(1)} copy(bf16[3,512,512]{2,1,0:T(8,128)(2,1)} %param.5) | data formatting | bytes 3145728 | tf_op args[0]
  1.8 4.7 %collective-permute-start = (bf16[3,2,512]{2,1,0:T(2,128)(2,1)S(1)}, bf16[3,2,512]{2,1,0:T(2,128)(2,1)S(1)}, u32[]{:S(2)}, u32[]{:S(2)}) collective-permute-start(bf16[3,2,512]{2,1,0:T(2,128)(2,1)S(1)} %slice_bitcast_fusion.5), channel_id=1, source_target_pairs={{0,16},{16,32},{32,48},{48,64},{64,80},{80,96},{96,112},{112,128},... | collective-permute-start | bytes 18440 | tf_op jit(solution)/shard_map/ppermute | solution.py:10
  6.4 3.9 %multiply_exponential_fusion = f32[512,16,128]{2,0,1:T(8,128)} fusion(f32[512,16]{0,1:T(8,128)} %param.8), kind=kLoop, calls=%fused_computation.10 | loop fusion | flops 1048576 | bytes 4227072 | tf_op jit(solution)/shard_map/exp | solution.py:51
  10.3 0.0 copy-done
  10.3 0.0 copy-done.2
  10.4 0.0 collective-permute-done
  10.4 0.5 maximum_convert_fusion
  10.9 0.9 fusion.7
  11.8 1.2 fusion.14
  13.0 2.5 %copy.26 = f32[512,4,128]{2,0,1:T(8,128)} copy(f32[512,4,128]{0,2,1:T(8,128)} %bitcast.77) | data formatting | bytes 2097152 | tf_op jit(solution)/shard_map/convert_element_type | solution.py:44
  15.5 0.0 copy-start.1
  15.5 6.4 %multiply_reduce_fusion = (f32[512,16,4]{0,2,1:T(4,128)S(1)}, bf16[512,16,4,128]{3,0,2,1:T(8,128)(2,1)S(1)}, bf16[512,16,4,128]{3,0,2,1:T(8,128)(2,1)S(1)}) fusion(f32[512,16,128]{2,0,1:T(8,128)} %multiply_exponential_fusion, f32[512,4,128]{2,0,1:T(8,128)} %copy.26), kind=kLoop, calls=%fused_computation | loop fusion | flops 25133056 | bytes 22151168 | tf_op jit(solution)/shard_map/reduce_sum | solution.py:64
  22.0 4.0 %collective-permute-start.1 = (f32[512,16]{0,1:T(8,128)S(1)}, f32[512,16]{0,1:T(8,128)S(1)}, u32[]{:S(2)}, u32[]{:S(2)}) collective-permute-start(f32[512,16]{0,1:T(8,128)S(1)} %get-tuple-element.8), channel_id=1, source_target_pairs={{0,16},{16,32},{32,48},{48,64},{64,80},{80,96},{96,112},{112,128},... | collective-permute-start | bytes 98312 | tf_op jit(solution)/shard_map/ppermute | solution.py:10
  26.1 3.8 %collective-permute-start.2 = (f32[512,16]{0,1:T(8,128)S(1)}, f32[512,16]{0,1:T(8,128)S(1)}, u32[]{:S(2)}, u32[]{:S(2)}) collective-permute-start(f32[512,16]{0,1:T(8,128)S(1)} %get-tuple-element.8), channel_id=1, source_target_pairs={{0,32},{16,48},{32,64},{48,80},{64,96},{80,112},{96,128},{112,144}... | collective-permute-start | bytes 98312 | tf_op jit(solution)/shard_map/ppermute | solution.py:10
  29.9 0.0 collective-permute-done.1
  29.9 1.6 %collective-permute-done.2 = f32[512,16]{0,1:T(8,128)S(1)} collective-permute-done((f32[512,16]{0,1:T(8,128)S(1)}, f32[512,16]{0,1:T(8,128)S(1)}, u32[]{:S(2)}, u32[]{:S(2)}) %collective-permute-start.2) | collective-permute-done | bytes 32800 | tf_op jit(solution)/shard_map/ppermute | solution.py:10
  31.5 4.2 %collective-permute-start.3 = (f32[512,16]{0,1:T(8,128)S(1)}, f32[512,16]{0,1:T(8,128)S(1)}, u32[]{:S(2)}, u32[]{:S(2)}) collective-permute-start(f32[512,16]{0,1:T(8,128)S(1)} %multiply_add_fusion.5), channel_id=1, source_target_pairs={{0,32},{16,48},{32,64},{48,80},{64,96},{80,112},{96,128},{112,144}... | collective-permute-start | bytes 98312 | tf_op jit(solution)/shard_map/ppermute | solution.py:10
  35.7 1.6 %collective-permute-done.3 = f32[512,16]{0,1:T(8,128)S(1)} collective-permute-done((f32[512,16]{0,1:T(8,128)S(1)}, f32[512,16]{0,1:T(8,128)S(1)}, u32[]{:S(2)}, u32[]{:S(2)}) %collective-permute-start.3) | collective-permute-done | bytes 32800 | tf_op jit(solution)/shard_map/ppermute | solution.py:10
  37.3 7.5 %collective-permute-start.4 = (f32[512,16]{0,1:T(8,128)S(1)}, f32[512,16]{0,1:T(8,128)S(1)}, u32[]{:S(2)}, u32[]{:S(2)}) collective-permute-start(f32[512,16]{0,1:T(8,128)S(1)} %multiply_add_fusion.4), channel_id=1, source_target_pairs={{0,64},{16,80},{32,96},{48,112},{64,128},{80,144},{96,160},{112,17... | collective-permute-start | bytes 98312 | tf_op jit(solution)/shard_map/ppermute | solution.py:10
  44.9 1.6 %collective-permute-done.4 = f32[512,16]{0,1:T(8,128)S(1)} collective-permute-done((f32[512,16]{0,1:T(8,128)S(1)}, f32[512,16]{0,1:T(8,128)S(1)}, u32[]{:S(2)}, u32[]{:S(2)}) %collective-permute-start.4) | collective-permute-done | bytes 32800 | tf_op jit(solution)/shard_map/ppermute | solution.py:10
  46.5 10.7 %collective-permute-start.5 = (f32[512,16]{0,1:T(8,128)S(1)}, f32[512,16]{0,1:T(8,128)S(1)}, u32[]{:S(2)}, u32[]{:S(2)}) collective-permute-start(f32[512,16]{0,1:T(8,128)S(1)} %multiply_add_fusion.3), channel_id=1, source_target_pairs={{0,128},{16,144},{32,160},{48,176},{64,192},{80,208},{96,224},{112... | collective-permute-start | bytes 98312 | tf_op jit(solution)/shard_map/ppermute | solution.py:10
  57.2 1.6 %collective-permute-done.5 = f32[512,16]{0,1:T(8,128)S(1)} collective-permute-done((f32[512,16]{0,1:T(8,128)S(1)}, f32[512,16]{0,1:T(8,128)S(1)}, u32[]{:S(2)}, u32[]{:S(2)}) %collective-permute-start.5) | collective-permute-done | bytes 32800 | tf_op jit(solution)/shard_map/ppermute | solution.py:10
  58.8 15.7 %collective-permute-start.6 = (f32[512,16]{0,1:T(8,128)S(1)}, f32[512,16]{0,1:T(8,128)S(1)}, u32[]{:S(2)}, u32[]{:S(2)}) collective-permute-start(f32[512,16]{0,1:T(8,128)S(1)} %multiply_add_fusion.2), channel_id=1, source_target_pairs={{0,256},{16,272},{32,288},{48,304},{64,320},{80,336},{96,352},{112... | collective-permute-start | bytes 98312 | tf_op jit(solution)/shard_map/ppermute | solution.py:10
  74.5 1.6 %collective-permute-done.6 = f32[512,16]{0,1:T(8,128)S(1)} collective-permute-done((f32[512,16]{0,1:T(8,128)S(1)}, f32[512,16]{0,1:T(8,128)S(1)}, u32[]{:S(2)}, u32[]{:S(2)}) %collective-permute-start.6) | collective-permute-done | bytes 32800 | tf_op jit(solution)/shard_map/ppermute | solution.py:10
  76.1 25.0 %collective-permute-start.7 = (f32[512,16]{0,1:T(8,128)S(1)}, f32[512,16]{0,1:T(8,128)S(1)}, u32[]{:S(2)}, u32[]{:S(2)}) collective-permute-start(f32[512,16]{0,1:T(8,128)S(1)} %multiply_add_fusion.1), channel_id=1, source_target_pairs={{0,512},{16,528},{32,544},{48,560},{64,576},{80,592},{96,608},{112... | collective-permute-start | bytes 98312 | tf_op jit(solution)/shard_map/ppermute | solution.py:10
  101.2 1.6 %collective-permute-done.7 = f32[512,16]{0,1:T(8,128)S(1)} collective-permute-done((f32[512,16]{0,1:T(8,128)S(1)}, f32[512,16]{0,1:T(8,128)S(1)}, u32[]{:S(2)}, u32[]{:S(2)}) %collective-permute-start.7) | collective-permute-done | bytes 32800 | tf_op jit(solution)/shard_map/ppermute | solution.py:10
  102.7 0.0 copy-done.1
  102.7 0.1 maximum_multiply_fusion
  102.8 0.1 copy.28
  102.9 2.3 %exponential_multiply_fusion = f32[512,16,128]{2,0,1:T(8,128)S(1)} fusion(f32[512,16]{0,1:T(8,128)S(1)} %get-tuple-element.15, f32[512,16]{0,1:T(8,128)S(1)} %get-tuple-element.14), kind=kLoop, calls=%fused_computation.11 | loop fusion | flops 2097152 | bytes 4259840 | tf_op jit(solution)/shard_map/mul | solution.py:52
  105.3 0.1 exponential_multiply_fusion.1
  105.4 5.1 %multiply_reduce_fusion.1 = f32[512,4,128]{2,0,1:T(8,128)S(1)} fusion(f32[512,16,4]{0,2,1:T(4,128)S(1)} %exponential_multiply_fusion.1, f32[512,16,128]{2,0,1:T(8,128)S(1)} %exponential_multiply_fusion), kind=kLoop, calls=%fused_computation.8 | loop fusion | flops 8126464 | bytes 5373952 | tf_op jit(solution)/shard_map/reduce_sum | solution.py:78
  110.5 7.9 %multiply_reduce_fusion.2 = f32[512,4,128]{2,0,1:T(8,128)S(1)} fusion(bf16[512,16,4,128]{3,0,2,1:T(8,128)(2,1)S(1)} %get-tuple-element.6, bf16[512,16,4,128]{3,0,2,1:T(8,128)(2,1)S(1)} %get-tuple-element.7, f32[512,16,4]{0,2,1:T(4,128)S(1)} %copy.28, f32[512,16,128]{2,0,1:T(8,128)S(1)} %exponential_multiply_fusion, pred[128,128]{1,0:T(32,128)(4,1)S(1)} %iota_compare_fusion), kind=kOutput, calls=%fused_computation.9 | convolution fusion | flops 2193391616 | bytes 22167552 | tf_op jit(solution)/shard_map/ckni,ij->cknj/dot_general | solution.py:62
  118.4 0.0 copy-start.3
  118.4 1.1 add.76
  119.5 2.5 %copy.29 = f32[512,4,128]{0,2,1:T(8,128)} copy(f32[512,4,128]{2,0,1:T(8,128)} %add.76) | data formatting | bytes 2097152 | tf_op jit(solution)/shard_map/add | solution.py:78
  122.1 0.0 copy-done.3
  122.1 2.5 %fusion.11 = bf16[512,512]{0,1:T(8,128)(2,1)} fusion(f32[3,512,512]{1,2,0:T(8,128)S(1)} %fusion.7, f32[512,4,128]{0,2,1:T(8,128)} %copy.29, f32[512]{0:T(512)S(1)} %copy-done.3), kind=kLoop, calls=%fused_computation.22 | loop fusion | flops 2359296 | bytes 4720640 | tf_op jit(solution)/shard_map/convert_element_type | solution.py:81
  124.6 2.0 %copy.30 = bf16[512,512]{1,0:T(8,128)(2,1)} copy(bf16[512,512]{0,1:T(8,128)(2,1)} %fusion.11) | data formatting | bytes 1048576 | tf_op jit(solution)/shard_map/convert_element_type | solution.py:81
  (16 shorter events, 0.2 us)
Async XLA Ops:
  0.0 10.3 %copy-start = (f32[512,16]{0,1:T(8,128)S(1)}, f32[512,16]{0,1:T(8,128)}, u32[]{:S(2)}) copy-start(f32[512,16]{0,1:T(8,128)} %param.8) | copy-start | bytes 98308
  0.0 10.3 %copy-start.2 = (f32[3,512,3]{1,2,0:T(4,128)S(1)}, f32[3,512,3]{1,2,0:T(4,128)}, u32[]{:S(2)}) copy-start(f32[3,512,3]{1,2,0:T(4,128)} %param.6) | copy-start | bytes 55300
  1.8 8.6 %collective-permute-start = (bf16[3,2,512]{2,1,0:T(2,128)(2,1)S(1)}, bf16[3,2,512]{2,1,0:T(2,128)(2,1)S(1)}, u32[]{:S(2)}, u32[]{:S(2)}) collective-permute-start(bf16[3,2,512]{2,1,0:T(2,128)(2,1)S(1)} %slice_bitcast_fusion.5), channel_id=1, source_target_pairs={{0,16},{16,32},{32,48},{48,64},{64,80},{80,96},{96,112},{112,128},... | collective-permute-start | bytes 18440 | tf_op jit(solution)/shard_map/ppermute | solution.py:10
  15.5 87.2 %copy-start.1 = (f32[512,16]{0,1:T(8,128)S(1)}, f32[512,16]{0,1:T(8,128)}, u32[]{:S(2)}) copy-start(f32[512,16]{0,1:T(8,128)} %param.9) | copy-start | bytes 98308
  22.0 7.9 %collective-permute-start.1 = (f32[512,16]{0,1:T(8,128)S(1)}, f32[512,16]{0,1:T(8,128)S(1)}, u32[]{:S(2)}, u32[]{:S(2)}) collective-permute-start(f32[512,16]{0,1:T(8,128)S(1)} %get-tuple-element.8), channel_id=1, source_target_pairs={{0,16},{16,32},{32,48},{48,64},{64,80},{80,96},{96,112},{112,128},... | collective-permute-start | bytes 98312 | tf_op jit(solution)/shard_map/ppermute | solution.py:10
  26.1 5.4 %collective-permute-start.2 = (f32[512,16]{0,1:T(8,128)S(1)}, f32[512,16]{0,1:T(8,128)S(1)}, u32[]{:S(2)}, u32[]{:S(2)}) collective-permute-start(f32[512,16]{0,1:T(8,128)S(1)} %get-tuple-element.8), channel_id=1, source_target_pairs={{0,32},{16,48},{32,64},{48,80},{64,96},{80,112},{96,128},{112,144}... | collective-permute-start | bytes 98312 | tf_op jit(solution)/shard_map/ppermute | solution.py:10
  31.5 5.8 %collective-permute-start.3 = (f32[512,16]{0,1:T(8,128)S(1)}, f32[512,16]{0,1:T(8,128)S(1)}, u32[]{:S(2)}, u32[]{:S(2)}) collective-permute-start(f32[512,16]{0,1:T(8,128)S(1)} %multiply_add_fusion.5), channel_id=1, source_target_pairs={{0,32},{16,48},{32,64},{48,80},{64,96},{80,112},{96,128},{112,144}... | collective-permute-start | bytes 98312 | tf_op jit(solution)/shard_map/ppermute | solution.py:10
  37.3 9.1 %collective-permute-start.4 = (f32[512,16]{0,1:T(8,128)S(1)}, f32[512,16]{0,1:T(8,128)S(1)}, u32[]{:S(2)}, u32[]{:S(2)}) collective-permute-start(f32[512,16]{0,1:T(8,128)S(1)} %multiply_add_fusion.4), channel_id=1, source_target_pairs={{0,64},{16,80},{32,96},{48,112},{64,128},{80,144},{96,160},{112,17... | collective-permute-start | bytes 98312 | tf_op jit(solution)/shard_map/ppermute | solution.py:10
  46.5 12.3 %collective-permute-start.5 = (f32[512,16]{0,1:T(8,128)S(1)}, f32[512,16]{0,1:T(8,128)S(1)}, u32[]{:S(2)}, u32[]{:S(2)}) collective-permute-start(f32[512,16]{0,1:T(8,128)S(1)} %multiply_add_fusion.3), channel_id=1, source_target_pairs={{0,128},{16,144},{32,160},{48,176},{64,192},{80,208},{96,224},{112... | collective-permute-start | bytes 98312 | tf_op jit(solution)/shard_map/ppermute | solution.py:10
  58.8 17.3 %collective-permute-start.6 = (f32[512,16]{0,1:T(8,128)S(1)}, f32[512,16]{0,1:T(8,128)S(1)}, u32[]{:S(2)}, u32[]{:S(2)}) collective-permute-start(f32[512,16]{0,1:T(8,128)S(1)} %multiply_add_fusion.2), channel_id=1, source_target_pairs={{0,256},{16,272},{32,288},{48,304},{64,320},{80,336},{96,352},{112... | collective-permute-start | bytes 98312 | tf_op jit(solution)/shard_map/ppermute | solution.py:10
  76.1 26.6 %collective-permute-start.7 = (f32[512,16]{0,1:T(8,128)S(1)}, f32[512,16]{0,1:T(8,128)S(1)}, u32[]{:S(2)}, u32[]{:S(2)}) collective-permute-start(f32[512,16]{0,1:T(8,128)S(1)} %multiply_add_fusion.1), channel_id=1, source_target_pairs={{0,512},{16,528},{32,544},{48,560},{64,576},{80,592},{96,608},{112... | collective-permute-start | bytes 98312 | tf_op jit(solution)/shard_map/ppermute | solution.py:10
  118.4 3.7 %copy-start.3 = (f32[512]{0:T(512)S(1)}, f32[512]{0:T(512)}, u32[]{:S(2)}) copy-start(f32[512]{0:T(512)} %param.7) | copy-start | bytes 6148

commit v3 on v2

--- a/solution.py
+++ b/solution.py
@@ -23,16 +23,43 @@
     return feats
 
 
+def moved(value, pairs):
+    return lax.ppermute(value, "seq", pairs)
+
+
 def scan_states(final, rate, length):
     count = lax.axis_size("seq")
-    acc = from_behind(final, "seq", 1)
-    if count > 2:
-        acc = acc + jnp.exp(-rate * length) * from_behind(final, "seq", 2)
-    shift = 2
-    while shift < count:
-        acc = acc + jnp.exp(-rate * float(length * shift)) * from_behind(acc, "seq", shift)
-        shift *= 2
-    return acc
+    ring = count // 2
+    half = ring // 2
+    here = lax.axis_index("seq")
+    z = here // 2
+    odd = here % 2
+    unit = jnp.exp(-rate * float(length))
+    partner = moved(final, [(d, d ^ 1) for d in range(count)])
+    first = jnp.where(odd == 1, partner, final)
+    second = jnp.where(odd == 1, final, partner)
+    pair = unit * first + second
+
+    def forward(value, steps):
+        pairs = [(d, d + 2 * steps) for d in range(count) if d + 2 * steps < count]
+        return moved(value, pairs) if pairs else jnp.zeros_like(value)
+
+    def backward(value, steps):
+        return moved(value, [(d, (d - 2 * steps) % count) for d in range(count)])
+
+    def decay(steps):
+        return jnp.exp(-rate * float(2 * length * steps))
+
+    near = forward(pair, 1) + decay(1) * forward(pair, 2)
+    far = jnp.where(z < half, pair, 0.0)
+    width = 1
+    while width < half:
+        near = near + decay(width * 2) * forward(near, width * 2) if width * 2 < half else near
+        far = decay(width) * far + backward(far, width)
+        width *= 2
+    near_done = near
+    whole = near_done + jnp.where(z > half, decay(half), 0.0) * far
+    return jnp.where(odd == 1, unit * whole + first, whole)
 
 
 def shards(projected, short_weight, skip_weight, decay_rates, residues):

time: 127 us -> 132 us (1.039)
  the two profiles are of different devices: /device:TPU:14 before, /device:TPU:2 now
where the time goes in v3:
time: 132 us
  starting transfers between devices  73.4 us (56%)
  other arithmetic  28.1 us (21%)
  waiting for transfers between devices  11.3 us (9%)
  matrix products  9.39 us (7%)
  local copies, waits for them, and re-layouts  9 us (7%)
    ppermute x10, starting transfers between devices, moved(): return lax.ppermute(value, 'seq', pairs)  69.3 us
    ppermute x10, waiting for transfers between devices, moved(): return lax.ppermute(value, 'seq', pairs)  11.3 us
    reduce_sum x1, other arithmetic, shards(): jnp.sum(scaled, axis=3) * jnp.exp(-rate * (block - 1))[:, :, None]  10.1 us
    dot_general x1, matrix products, shards(): jnp.einsum('ckni,ij->cknj', pair, stacked, preferred_element_type=jnp.flo...  9.39 us
    reduce_sum x1, other arithmetic, shards(): jnp.sum(falling[:, :, None, :] * entering[:, :, :, None], axis=1)  5.08 us
    ppermute x1, starting transfers between devices, from_behind(): lax.ppermute(value, axis, [(source, source + steps) for source in range(l...  4.03 us
    exp x1, other arithmetic, shards(): rising = jnp.exp(rate[:, :, None] * offsets)  3.92 us
  transfers between devices with their start and end apart: 11, of which 6 were waited for; matrix products, arithmetic and copies ran while one was open for 3% of the time, Pallas kernels for 0%

profile of v3, /device:TPU:2, one launch (start us, length us, event | category | flops | bytes accessed | tf_op | source)
XLA Modules:
  0.0 131.5 jit_solution(6196910708762062747)
XLA Ops:
  0.0 0.0 copy-start.1
  0.0 0.0 copy-start.3
  0.0 1.7 %copy.24 = bf16[3,512,512]{1,2,0:T(8,128)(2,1)S(1)} copy(bf16[3,512,512]{2,1,0:T(8,128)(2,1)} %param.5) | data formatting | bytes 3145728 | tf_op args[0]
  1.8 4.0 %collective-permute-start = (bf16[3,2,512]{2,1,0:T(2,128)(2,1)S(1)}, bf16[3,2,512]{2,1,0:T(2,128)(2,1)S(1)}, u32[]{:S(2)}, u32[]{:S(2)}) collective-permute-start(bf16[3,2,512]{2,1,0:T(2,128)(2,1)S(1)} %slice_bitcast_fusion.5), channel_id=1, source_target_pairs={{0,16},{16,32},{32,48},{48,64},{64,80},{80,96},{96,112},{112,128},... | collective-permute-start | bytes 18440 | tf_op jit(solution)/shard_map/ppermute | solution.py:10
  5.8 3.9 %multiply_exponential_fusion = f32[512,16,128]{2,0,1:T(8,128)} fusion(f32[512,16]{0,1:T(8,128)} %param.8), kind=kLoop, calls=%fused_computation.10 | loop fusion | flops 1048576 | bytes 4227072 | tf_op jit(solution)/shard_map/exp | solution.py:78
  9.7 0.0 copy-done.1
  9.7 0.0 copy-done.3
  9.8 0.0 collective-permute-done
  9.8 0.5 maximum_convert_fusion
  10.3 0.9 fusion.7
  11.2 1.2 fusion.14
  12.4 2.5 %copy.26 = f32[512,4,128]{2,0,1:T(8,128)} copy(f32[512,4,128]{0,2,1:T(8,128)} %bitcast.77) | data formatting | bytes 2097152 | tf_op jit(solution)/shard_map/convert_element_type | solution.py:71
  14.9 0.0 copy-start.2
  14.9 10.1 %multiply_reduce_fusion = (f32[512,16,4]{0,2,1:T(4,128)S(1)}, bf16[512,16,4,128]{3,0,2,1:T(8,128)(2,1)}, bf16[512,16,4,128]{3,0,2,1:T(8,128)(2,1)}) fusion(f32[512,16,128]{2,0,1:T(8,128)} %multiply_exponential_fusion, f32[512,4,128]{2,0,1:T(8,128)} %copy.26), kind=kLoop, calls=%fused_computation | loop fusion | flops 25133056 | bytes 22151168 | tf_op jit(solution)/shard_map/reduce_sum | solution.py:91
  25.1 4.7 %collective-permute-start.1 = (f32[512,16]{0,1:T(8,128)S(1)}, f32[512,16]{0,1:T(8,128)S(1)}, u32[]{:S(2)}, u32[]{:S(2)}) collective-permute-start(f32[512,16]{0,1:T(8,128)S(1)} %get-tuple-element.10), channel_id=1, source_target_pairs={{0,16},{16,0},{32,48},{48,32},{64,80},{80,64},{96,112},{112,96},{1... | collective-permute-start | bytes 98312 | tf_op jit(solution)/shard_map/ppermute | solution.py:27
  29.8 2.6 %collective-permute-done.1 = f32[512,16]{0,1:T(8,128)S(1)} collective-permute-done((f32[512,16]{0,1:T(8,128)S(1)}, f32[512,16]{0,1:T(8,128)S(1)}, u32[]{:S(2)}, u32[]{:S(2)}) %collective-permute-start.1) | collective-permute-done | bytes 32800 | tf_op jit(solution)/shard_map/ppermute | solution.py:27
  32.4 3.8 %collective-permute-start.2 = (f32[512,16]{0,1:T(8,128)S(1)}, f32[512,16]{0,1:T(8,128)S(1)}, u32[]{:S(2)}, u32[]{:S(2)}) collective-permute-start(f32[512,16]{0,1:T(8,128)S(1)} %get-tuple-element.6), channel_id=1, source_target_pairs={{0,32},{16,48},{32,64},{48,80},{64,96},{80,112},{96,128},{112,144}... | collective-permute-start | bytes 98312 | tf_op jit(solution)/shard_map/ppermute | solution.py:27
  36.3 5.6 %collective-permute-start.3 = (f32[512,16]{0,1:T(8,128)S(1)}, f32[512,16]{0,1:T(8,128)S(1)}, u32[]{:S(2)}, u32[]{:S(2)}) collective-permute-start(f32[512,16]{0,1:T(8,128)S(1)} %get-tuple-element.6), channel_id=1, source_target_pairs={{0,64},{16,80},{32,96},{48,112},{64,128},{80,144},{96,160},{112,17... | collective-permute-start | bytes 98312 | tf_op jit(solution)/shard_map/ppermute | solution.py:27
  41.9 0.0 collective-permute-done.2
  41.9 1.6 %collective-permute-done.3 = f32[512,16]{0,1:T(8,128)S(1)} collective-permute-done((f32[512,16]{0,1:T(8,128)S(1)}, f32[512,16]{0,1:T(8,128)S(1)}, u32[]{:S(2)}, u32[]{:S(2)}) %collective-permute-start.3) | collective-permute-done | bytes 32800 | tf_op jit(solution)/shard_map/ppermute | solution.py:27
  43.5 5.9 %collective-permute-start.4 = (f32[512,16]{0,1:T(8,128)S(1)}, f32[512,16]{0,1:T(8,128)S(1)}, u32[]{:S(2)}, u32[]{:S(2)}) collective-permute-start(f32[512,16]{0,1:T(8,128)S(1)} %multiply_add_fusion.5), channel_id=1, source_target_pairs={{0,64},{16,80},{32,96},{48,112},{64,128},{80,144},{96,160},{112,17... | collective-permute-start | bytes 98312 | tf_op jit(solution)/shard_map/ppermute | solution.py:27
  49.4 11.2 %collective-permute-start.7 = (f32[512,16]{0,1:T(8,128)S(1)}, f32[512,16]{0,1:T(8,128)S(1)}, u32[]{:S(2)}, u32[]{:S(2)}) collective-permute-start(f32[512,16]{0,1:T(8,128)S(1)} %get-tuple-element.5), channel_id=1, source_target_pairs={{0,992},{16,1008},{32,0},{48,16},{64,32},{80,48},{96,64},{112,80},... | collective-permute-start | bytes 98312 | tf_op jit(solution)/shard_map/ppermute | solution.py:27
  60.6 0.0 collective-permute-done.4
  60.7 2.2 %collective-permute-start.5 = (f32[512,16]{0,1:T(8,128)S(1)}, f32[512,16]{0,1:T(8,128)S(1)}, u32[]{:S(2)}, u32[]{:S(2)}) collective-permute-start(f32[512,16]{0,1:T(8,128)S(1)} %multiply_add_fusion.4), channel_id=1, source_target_pairs={{0,128},{16,144},{32,160},{48,176},{64,192},{80,208},{96,224},{112... | collective-permute-start | bytes 98312 | tf_op jit(solution)/shard_map/ppermute | solution.py:27
  62.9 0.0 collective-permute-done.7
  62.9 1.6 %collective-permute-done.5 = f32[512,16]{0,1:T(8,128)S(1)} collective-permute-done((f32[512,16]{0,1:T(8,128)S(1)}, f32[512,16]{0,1:T(8,128)S(1)}, u32[]{:S(2)}, u32[]{:S(2)}) %collective-permute-start.5) | collective-permute-done | bytes 32800 | tf_op jit(solution)/shard_map/ppermute | solution.py:27
  64.5 13.2 %collective-permute-start.8 = (f32[512,16]{0,1:T(8,128)S(1)}, f32[512,16]{0,1:T(8,128)S(1)}, u32[]{:S(2)}, u32[]{:S(2)}) collective-permute-start(f32[512,16]{0,1:T(8,128)S(1)} %get-tuple-element.19), channel_id=1, source_target_pairs={{0,960},{16,976},{32,992},{48,1008},{64,0},{80,16},{96,32},{112,48... | collective-permute-start | bytes 98312 | tf_op jit(solution)/shard_map/ppermute | solution.py:27
  77.7 1.6 %collective-permute-done.8 = f32[512,16]{0,1:T(8,128)S(1)} collective-permute-done((f32[512,16]{0,1:T(8,128)S(1)}, f32[512,16]{0,1:T(8,128)S(1)}, u32[]{:S(2)}, u32[]{:S(2)}) %collective-permute-start.8) | collective-permute-done | bytes 32800 | tf_op jit(solution)/shard_map/ppermute | solution.py:27
  79.3 9.7 %collective-permute-start.9 = (f32[512,16]{0,1:T(8,128)S(1)}, f32[512,16]{0,1:T(8,128)S(1)}, u32[]{:S(2)}, u32[]{:S(2)}) collective-permute-start(f32[512,16]{0,1:T(8,128)S(1)} %multiply_add_fusion.1), channel_id=1, source_target_pairs={{0,896},{16,912},{32,928},{48,944},{64,960},{80,976},{96,992},{112... | collective-permute-start | bytes 98312 | tf_op jit(solution)/shard_map/ppermute | solution.py:27
  89.0 1.3 collective-permute-start.6
  90.3 0.3 collective-permute-done.9
  90.6 11.7 %collective-permute-start.10 = (f32[512,16]{0,1:T(8,128)S(1)}, f32[512,16]{0,1:T(8,128)S(1)}, u32[]{:S(2)}, u32[]{:S(2)}) collective-permute-start(f32[512,16]{0,1:T(8,128)S(1)} %multiply_add_fusion), channel_id=1, source_target_pairs={{0,768},{16,784},{32,800},{48,816},{64,832},{80,848},{96,864},{112... | collective-permute-start | bytes 98312 | tf_op jit(solution)/shard_map/ppermute | solution.py:27
  102.3 0.0 collective-permute-done.6
  102.3 3.7 %collective-permute-done.10 = f32[512,16]{0,1:T(8,128)S(1)} collective-permute-done((f32[512,16]{0,1:T(8,128)S(1)}, f32[512,16]{0,1:T(8,128)S(1)}, u32[]{:S(2)}, u32[]{:S(2)}) %collective-permute-start.10) | collective-permute-done | bytes 32800 | tf_op jit(solution)/shard_map/ppermute | solution.py:27
  106.1 0.0 copy-done.2
  106.1 0.1 maximum_multiply_fusion
  106.2 0.1 copy.28
  106.3 0.0 copy-start
  106.3 2.3 %exponential_multiply_fusion = f32[512,16,128]{2,0,1:T(8,128)S(1)} fusion(f32[512,16]{0,1:T(8,128)S(1)} %get-tuple-element.17, f32[512,16]{0,1:T(8,128)S(1)} %get-tuple-element.16), kind=kLoop, calls=%fused_computation.11 | loop fusion | flops 2097152 | bytes 4259840 | tf_op jit(solution)/shard_map/mul | solution.py:79
  108.6 0.1 exponential_multiply_fusion.1
  108.7 5.1 %multiply_reduce_fusion.1 = f32[512,4,128]{2,0,1:T(8,128)S(1)} fusion(f32[512,16,4]{0,2,1:T(4,128)S(1)} %exponential_multiply_fusion.1, f32[512,16,128]{2,0,1:T(8,128)S(1)} %exponential_multiply_fusion), kind=kLoop, calls=%fused_computation.8 | loop fusion | flops 8126464 | bytes 5373952 | tf_op jit(solution)/shard_map/reduce_sum | solution.py:105
  113.8 0.0 copy-done
  113.8 9.4 %multiply_reduce_fusion.2 = f32[512,4,128]{2,0,1:T(8,128)S(1)} fusion(bf16[512,16,4,128]{3,0,2,1:T(8,128)(2,1)S(1)} %copy-done, bf16[512,16,4,128]{3,0,2,1:T(8,128)(2,1)} %get-tuple-element.9, f32[512,16,4]{0,2,1:T(4,128)S(1)} %copy.28, f32[512,16,128]{2,0,1:T(8,128)S(1)} %exponential_multiply_fusion, pred[128,128]{1,0:T(32,128)(4,1)S(1)} %iota_compare_fusion), kind=kOutput, calls=%fused_computation.9 | convolution fusion | flops 2193391616 | bytes 22167552 | tf_op jit(solution)/shard_map/ckni,ij->cknj/dot_general | solution.py:89
  123.2 0.0 copy-start.4
  123.3 1.1 add.102
  124.4 2.5 %copy.29 = f32[512,4,128]{0,2,1:T(8,128)} copy(f32[512,4,128]{2,0,1:T(8,128)} %add.102) | data formatting | bytes 2097152 | tf_op jit(solution)/shard_map/add | solution.py:105
  126.9 0.0 copy-done.4
  126.9 2.6 %fusion.11 = bf16[512,512]{0,1:T(8,128)(2,1)} fusion(f32[3,512,512]{1,2,0:T(8,128)S(1)} %fusion.7, f32[512,4,128]{0,2,1:T(8,128)} %copy.29, f32[512]{0:T(512)S(1)} %copy-done.4), kind=kLoop, calls=%fused_computation.22 | loop fusion | flops 2359296 | bytes 4720640 | tf_op jit(solution)/shard_map/convert_element_type | solution.py:108
  129.5 2.0 %copy.30 = bf16[512,512]{1,0:T(8,128)(2,1)} copy(bf16[512,512]{0,1:T(8,128)(2,1)} %fusion.11) | data formatting | bytes 1048576 | tf_op jit(solution)/shard_map/convert_element_type | solution.py:108
  (17 shorter events, 0.3 us)
Async XLA Ops:
  0.0 9.7 %copy-start.1 = (f32[512,16]{0,1:T(8,128)S(1)}, f32[512,16]{0,1:T(8,128)}, u32[]{:S(2)}) copy-start(f32[512,16]{0,1:T(8,128)} %param.8) | copy-start | bytes 98308
  0.0 9.7 %copy-start.3 = (f32[3,512,3]{1,2,0:T(4,128)S(1)}, f32[3,512,3]{1,2,0:T(4,128)}, u32[]{:S(2)}) copy-start(f32[3,512,3]{1,2,0:T(4,128)} %param.6) | copy-start | bytes 55300
  1.8 8.0 %collective-permute-start = (bf16[3,2,512]{2,1,0:T(2,128)(2,1)S(1)}, bf16[3,2,512]{2,1,0:T(2,128)(2,1)S(1)}, u32[]{:S(2)}, u32[]{:S(2)}) collective-permute-start(bf16[3,2,512]{2,1,0:T(2,128)(2,1)S(1)} %slice_bitcast_fusion.5), channel_id=1, source_target_pairs={{0,16},{16,32},{32,48},{48,64},{64,80},{80,96},{96,112},{112,128},... | collective-permute-start | bytes 18440 | tf_op jit(solution)/shard_map/ppermute | solution.py:10
  14.9 91.1 %copy-start.2 = (f32[512,16]{0,1:T(8,128)S(1)}, f32[512,16]{0,1:T(8,128)}, u32[]{:S(2)}) copy-start(f32[512,16]{0,1:T(8,128)} %param.9) | copy-start | bytes 98308
  25.1 7.3 %collective-permute-start.1 = (f32[512,16]{0,1:T(8,128)S(1)}, f32[512,16]{0,1:T(8,128)S(1)}, u32[]{:S(2)}, u32[]{:S(2)}) collective-permute-start(f32[512,16]{0,1:T(8,128)S(1)} %get-tuple-element.10), channel_id=1, source_target_pairs={{0,16},{16,0},{32,48},{48,32},{64,80},{80,64},{96,112},{112,96},{1... | collective-permute-start | bytes 98312 | tf_op jit(solution)/shard_map/ppermute | solution.py:27
  32.4 9.5 %collective-permute-start.2 = (f32[512,16]{0,1:T(8,128)S(1)}, f32[512,16]{0,1:T(8,128)S(1)}, u32[]{:S(2)}, u32[]{:S(2)}) collective-permute-start(f32[512,16]{0,1:T(8,128)S(1)} %get-tuple-element.6), channel_id=1, source_target_pairs={{0,32},{16,48},{32,64},{48,80},{64,96},{80,112},{96,128},{112,144}... | collective-permute-start | bytes 98312 | tf_op jit(solution)/shard_map/ppermute | solution.py:27
  36.3 7.2 %collective-permute-start.3 = (f32[512,16]{0,1:T(8,128)S(1)}, f32[512,16]{0,1:T(8,128)S(1)}, u32[]{:S(2)}, u32[]{:S(2)}) collective-permute-start(f32[512,16]{0,1:T(8,128)S(1)} %get-tuple-element.6), channel_id=1, source_target_pairs={{0,64},{16,80},{32,96},{48,112},{64,128},{80,144},{96,160},{112,17... | collective-permute-start | bytes 98312 | tf_op jit(solution)/shard_map/ppermute | solution.py:27
  43.5 17.1 %collective-permute-start.4 = (f32[512,16]{0,1:T(8,128)S(1)}, f32[512,16]{0,1:T(8,128)S(1)}, u32[]{:S(2)}, u32[]{:S(2)}) collective-permute-start(f32[512,16]{0,1:T(8,128)S(1)} %multiply_add_fusion.5), channel_id=1, source_target_pairs={{0,64},{16,80},{32,96},{48,112},{64,128},{80,144},{96,160},{112,17... | collective-permute-start | bytes 98312 | tf_op jit(solution)/shard_map/ppermute | solution.py:27
  49.4 13.5 %collective-permute-start.7 = (f32[512,16]{0,1:T(8,128)S(1)}, f32[512,16]{0,1:T(8,128)S(1)}, u32[]{:S(2)}, u32[]{:S(2)}) collective-permute-start(f32[512,16]{0,1:T(8,128)S(1)} %get-tuple-element.5), channel_id=1, source_target_pairs={{0,992},{16,1008},{32,0},{48,16},{64,32},{80,48},{96,64},{112,80},... | collective-permute-start | bytes 98312 | tf_op jit(solution)/shard_map/ppermute | solution.py:27
  60.7 3.8 %collective-permute-start.5 = (f32[512,16]{0,1:T(8,128)S(1)}, f32[512,16]{0,1:T(8,128)S(1)}, u32[]{:S(2)}, u32[]{:S(2)}) collective-permute-start(f32[512,16]{0,1:T(8,128)S(1)} %multiply_add_fusion.4), channel_id=1, source_target_pairs={{0,128},{16,144},{32,160},{48,176},{64,192},{80,208},{96,224},{112... | collective-permute-start | bytes 98312 | tf_op jit(solution)/shard_map/ppermute | solution.py:27
  64.5 14.8 %collective-permute-start.8 = (f32[512,16]{0,1:T(8,128)S(1)}, f32[512,16]{0,1:T(8,128)S(1)}, u32[]{:S(2)}, u32[]{:S(2)}) collective-permute-start(f32[512,16]{0,1:T(8,128)S(1)} %get-tuple-element.19), channel_id=1, source_target_pairs={{0,960},{16,976},{32,992},{48,1008},{64,0},{80,16},{96,32},{112,48... | collective-permute-start | bytes 98312 | tf_op jit(solution)/shard_map/ppermute | solution.py:27
  79.3 11.3 %collective-permute-start.9 = (f32[512,16]{0,1:T(8,128)S(1)}, f32[512,16]{0,1:T(8,128)S(1)}, u32[]{:S(2)}, u32[]{:S(2)}) collective-permute-start(f32[512,16]{0,1:T(8,128)S(1)} %multiply_add_fusion.1), channel_id=1, source_target_pairs={{0,896},{16,912},{32,928},{48,944},{64,960},{80,976},{96,992},{112... | collective-permute-start | bytes 98312 | tf_op jit(solution)/shard_map/ppermute | solution.py:27
  89.0 13.3 %collective-permute-start.6 = (f32[512,16]{0,1:T(8,128)S(1)}, f32[512,16]{0,1:T(8,128)S(1)}, u32[]{:S(2)}, u32[]{:S(2)}) collective-permute-start(f32[512,16]{0,1:T(8,128)S(1)} %get-tuple-element.18), channel_id=1, source_target_pairs={{0,256},{16,272},{32,288},{48,304},{64,320},{80,336},{96,352},{112... | collective-permute-start | bytes 98312 | tf_op jit(solution)/shard_map/ppermute | solution.py:27
  90.6 15.5 %collective-permute-start.10 = (f32[512,16]{0,1:T(8,128)S(1)}, f32[512,16]{0,1:T(8,128)S(1)}, u32[]{:S(2)}, u32[]{:S(2)}) collective-permute-start(f32[512,16]{0,1:T(8,128)S(1)} %multiply_add_fusion), channel_id=1, source_target_pairs={{0,768},{16,784},{32,800},{48,816},{64,832},{80,848},{96,864},{112... | collective-permute-start | bytes 98312 | tf_op jit(solution)/shard_map/ppermute | solution.py:27
  106.3 7.6 %copy-start = (bf16[512,16,4,128]{3,0,2,1:T(8,128)(2,1)S(1)}, bf16[512,16,4,128]{3,0,2,1:T(8,128)(2,1)}, u32[]{:S(2)}) copy-start(bf16[512,16,4,128]{3,0,2,1:T(8,128)(2,1)} %get-tuple-element.8) | copy-start | bytes 25165828
  123.2 3.7 %copy-start.4 = (f32[512]{0:T(512)S(1)}, f32[512]{0:T(512)}, u32[]{:S(2)}) copy-start(f32[512]{0:T(512)} %param.7) | copy-start | bytes 6148
